TPU v7x, 32 devices: a whole 2x2x4 slice. The times are simulated.
32 devices in a mesh: band: 8 (over y, x, core), date: 4 (over z).
Axes of the slice: x: 2, y: 2, z: 4, core: 2. Of those that a mesh axis runs over, the one named last changes fastest.
Arguments:
- inputs: bfloat16 [8, 32, 128, 512], P('date', 'band'), may hold values from -6 to 6
- preact_one: bfloat16 [8, 32, 128, 512], P('date', 'band'), may hold values from -8 to 8
- preact_two: bfloat16 [8, 32, 128, 512], P('date', 'band'), may hold values from -8 to 8
- cotangent: bfloat16 [8, 32, 128, 512], P('date', 'band'), may hold values from -6 to 6
- weight_one: bfloat16 [3, 3, 512, 512], replicated, may hold values from -0.09375 to 0.09375
- weight_two: bfloat16 [3, 3, 512, 512], replicated, may hold values from -0.09375 to 0.09375
Outputs:
- input_grad: bfloat16 [8, 32, 128, 512], P('date', 'band')
- weight_grad_one: float32 [4608, 512], P('date')
- weight_grad_two: float32 [4608, 512], P('date')
All inputs are finite; a program needn't handle non-finite values.
Results may differ from a plain program's by a relative error of at most 0.0057.
Values may be sent and summed in bfloat16 or wider, within the bound.
No kernel may reach another device: no remote copies, remote signals or barrier semaphores. Data moves between devices by JAX's collectives and lax.ppermute only.
A program may use at most 128 MiB of HBM per device.

v0:
```python
import jax
import jax.numpy as jnp
from jax import lax
from jax.sharding import PartitionSpec as P


def extended(array, sides, width):
    for axis, dim in sides:
        peers, length = (lax.axis_size(axis), array.shape[dim])
        up = [(i, (i + 1) % peers) for i in range(peers - 1)]
        down = [(j, i) for i, j in up]
        last = lax.slice_in_dim(array, length - width, length, axis=dim)
        leading = lax.slice_in_dim(array, 0, width, axis=dim)
        before = lax.ppermute(last, axis, up)
        after = lax.ppermute(leading, axis, down)
        array = jnp.concatenate([before, array, after], axis=dim)
    return array


def slope(field_value):
    logistic = jax.nn.sigmoid(field_value)
    return logistic * (1.0 + field_value * (1.0 - logistic))


def pad_columns(field_value):
    return jnp.pad(field_value, ((0, 0), (0, 0), (1, 1), (0, 0)))


def shifted(padded, row_offset, col_offset, row_count, rim_start):
    col_count = padded.shape[2] - 2
    return padded[
        :,
        rim_start - row_offset : rim_start - row_offset + row_count,
        1 - col_offset : 1 - col_offset + col_count,
        :,
    ]


def weight_terms(left_field, padded, rim_start, grad_scale):
    row_count = left_field.shape[1]
    tap_list = []
    for row_offset in (-1, 0, 1):
        for col_offset in (-1, 0, 1):
            shifted_piece = shifted(padded, row_offset, col_offset, row_count, rim_start)
            tap_list.append(
                lax.dot_general(
                    left_field,
                    shifted_piece,
                    (((0, 1, 2), (0, 1, 2)), ((), ())),
                    preferred_element_type=jnp.float32,
                )
            )
    stacked = jnp.stack(tap_list)
    return (stacked * grad_scale).reshape(-1, stacked.shape[2])


def back_terms(padded, weight, row_count, rim_start):
    accumulated = None
    for row_offset in (-1, 0, 1):
        for col_offset in (-1, 0, 1):
            shifted_piece = shifted(padded, row_offset, col_offset, row_count, rim_start)
            product = lax.dot_general(
                shifted_piece,
                weight[row_offset + 1, col_offset + 1],
                (((3,), (1,)), ((), ())),
                preferred_element_type=jnp.float32,
            )
            accumulated = product if accumulated is None else accumulated + product
    return accumulated


def settle(grad_term):
    share_rows = lax.psum_scatter(grad_term, "date", scatter_dimension=0, tiled=True)
    return lax.psum(share_rows, "band")


def body(inputs, preact_one, preact_two, cotangent, weight_one, weight_two):
    row_count = inputs.shape[1]
    grad_scale = 1.0 / (inputs.shape[0] * lax.axis_size("date"))
    act_one = jax.nn.silu(preact_one.astype(jnp.float32)).astype(jnp.bfloat16)
    delta_two = (cotangent.astype(jnp.float32) * slope(preact_two.astype(jnp.float32))).astype(
        jnp.bfloat16
    )
    padded_two = pad_columns(extended(delta_two, (("band", 1),), 1))
    term_two = weight_terms(act_one, padded_two, 1, grad_scale)
    grad_two = settle(term_two)
    back_one = back_terms(padded_two, weight_two, row_count, 1)
    delta_one = (back_one * slope(preact_one.astype(jnp.float32))).astype(jnp.bfloat16)
    padded_one = pad_columns(extended(delta_one, (("band", 1),), 1))
    term_one = weight_terms(inputs, padded_one, 1, grad_scale)
    grad_one = settle(term_one)
    input_grad = back_terms(padded_one, weight_one, row_count, 1).astype(jnp.bfloat16)
    return (input_grad, grad_one, grad_two)


def solution(mesh):
    placed = (
        P("date", "band", None, None),
        P("date", "band", None, None),
        P("date", "band", None, None),
        P("date", "band", None, None),
        P(),
        P(),
    )
    return jax.shard_map(
        body,
        mesh=mesh,
        in_specs=placed,
        out_specs=(P("date", "band", None, None), P("date", None), P("date", None)),
        check_vma=False,
    )
```

profile of v0, /device:TPU:0, one launch (start us, length us, event | category | flops | bytes accessed | tf_op | source)
XLA Modules:
  0.0 464.7 jit_solution(12425122409398483117)
XLA Ops:
  7.2 2.5 fusion.7
  9.8 1.4 collective-permute-start.1
  11.2 3.0 collective-permute-start
  23.6 4.8 %broadcast_multiply_fusion = f32[9,512,512]{2,1,0:T(8,128)} fusion(f32[9,512,512]{2,1,0:T(8,128)S(1)} %fusion.23), kind=kLoop, calls=%fused_computation.2 | loop fusion | flops 2359296 | bytes 18874368 | tf_op jit(solution)/shard_map/mul | solution.py:54
  28.7 2.2 fusion.109
  31.0 1.8 fusion.43
  32.8 1.8 fusion.39
  38.9 1.7 fusion.14
  42.0 7.8 %collective-permute-start.2 = (bf16[2,1,128,512]{3,2,1,0:T(8,128)(2,1)S(1)}, bf16[2,1,128,512]{3,2,1,0:T(8,128)(2,1)S(1)}, u32[]{:S(2)}, u32[]{:S(2)}) collective-permute-start(bf16[2,1,128,512]{3,2,1,0:T(8,128)(2,1)S(1)} %get-tuple-element.6), channel_id=1, source_target_pairs={{0,4},{4,8},{8,12},{12,16},{16,20},{20,24},{24,28},{1,5},{5,9},{9,... | collective-permute-start | bytes 786440 | tf_op jit(solution)/shard_map/ppermute | solution.py:14
  58.0 4.8 %broadcast_multiply_fusion.1 = f32[9,512,512]{2,1,0:T(8,128)} fusion(f32[9,512,512]{2,1,0:T(8,128)S(1)} %fusion.32), kind=kLoop, calls=%fused_computation.3 | loop fusion | flops 2359296 | bytes 18874368 | tf_op jit(solution)/shard_map/mul | solution.py:54
  63.1 3.6 fusion.99
  66.7 3.1 fusion.93
  69.8 3.1 fusion.59
  72.9 124.7 %reduce-scatter.5.cloned.1.call-done = f32[1152,512]{1,0:T(8,128)} async-done(((f32[4608,512]{1,0:T(8,128)}), f32[1152,512]{1,0:T(8,128)}) %reduce-scatter.5.cloned.1.call-update) | async-done | bytes 2359312 | tf_op jit(solution)/shard_map/reduce_scatter | solution.py:73
  197.6 164.5 %reduce-scatter.3.cloned.1.call-done = f32[1152,512]{1,0:T(8,128)} async-done(((f32[4608,512]{1,0:T(8,128)}), f32[1152,512]{1,0:T(8,128)}) %reduce-scatter.3.cloned.1.call-update) | async-done | bytes 2359312 | tf_op jit(solution)/shard_map/reduce_scatter | solution.py:73
  362.1 2.0 fusion.94
  364.1 1.8 fusion.62
  365.9 1.8 fusion.65
  367.7 1.9 fusion.68
  369.7 1.9 fusion.71
  372.4 3.2 add_convert_fusion
  375.6 77.7 %all-reduce.5.cloned.1.call-done = (f32[1152,512]{1,0:T(8,128)}, f32[1152,512]{1,0:T(8,128)}) async-done(((f32[1152,512]{1,0:T(8,128)}, f32[1152,512]{1,0:T(8,128)}), (f32[1152,512]{1,0:T(8,128)}, f32[1152,512]{1,0:T(8,128)})) %all-reduce.5.cloned.1.call-update) | async-done | bytes 4718608 | tf_op jit(solution)/shard_map/psum | solution.py:74
  453.3 3.4 copy.99
  456.8 1.4 copy.100
  (65 shorter events, 24.4 us)
Async XLA Ops:
  7.2 43.9 %copy-start = (bf16[2,4,128,512]{3,2,1,0:T(8,128)(2,1)S(1)}, bf16[2,4,128,512]{3,2,1,0:T(8,128)(2,1)}, u32[]{:S(2)}) copy-start(bf16[2,4,128,512]{3,2,1,0:T(8,128)(2,1)} %param.6) | copy-start | bytes 3145732
  7.2 190.4 %reduce-scatter.5.cloned.1.call-start = ((), (), s32[]{:S(2)}) async-start(), calls=%async_computation.3 | async-start | bytes 11796480 | tf_op jit(solution)/shard_map/reduce_scatter | solution.py:73
  9.7 12.3 %copy-start.3 = (bf16[2,4,128,512]{3,2,1,0:T(8,128)(2,1)}, bf16[2,4,128,512]{3,2,1,0:T(8,128)(2,1)S(1)}, u32[]{:S(2)}) copy-start(bf16[2,4,128,512]{3,2,1,0:T(8,128)(2,1)S(1)} %fusion.7) | copy-start | bytes 3145732
  9.7 6.1 %copy-start.9 = (bf16[2,4,128,512]{3,2,1,0:T(8,128)(2,1)S(1)}, bf16[2,4,128,512]{3,2,1,0:T(8,128)(2,1)}, u32[]{:S(2)}) copy-start(bf16[2,4,128,512]{3,2,1,0:T(8,128)(2,1)} %param.7) | copy-start | bytes 3145732
  9.8 4.5 collective-permute-start.1
  11.2 4.2 collective-permute-start
  28.5 333.6 %reduce-scatter.3.cloned.1.call-start = ((), (), s32[]{:S(2)}) async-start(), calls=%async_computation.2 | async-start | bytes 11796480 | tf_op jit(solution)/shard_map/reduce_scatter | solution.py:73
  28.7 2.3 copy-start.4
  28.7 5.9 %slice-start = ((s8[4718592]{0:T(1024)(128)(4,1)}), s8[4194304]{0:T(1024)(128)(4,1)S(1)}, s32[]{:S(2)}) async-start(s8[4718592]{0:T(1024)(128)(4,1)} %bitcast.305), calls=%async_computation.5 | async-start | bytes 8388608
  31.0 3.6 slice-start.1
  37.6 1.2 copy-start.10
  40.6 15.8 %copy-start.1 = (bf16[2,4,128,512]{3,2,1,0:T(8,128)(2,1)}, bf16[2,4,128,512]{3,2,1,0:T(8,128)(2,1)S(1)}, u32[]{:S(2)}) copy-start(bf16[2,4,128,512]{3,2,1,0:T(8,128)(2,1)S(1)} %fusion.14) | copy-start | bytes 3145732
  40.7 9.1 %collective-permute-start.3 = (bf16[2,1,128,512]{3,2,1,0:T(8,128)(2,1)S(1)}, bf16[2,1,128,512]{3,2,1,0:T(8,128)(2,1)S(1)}, u32[]{:S(2)}, u32[]{:S(2)}) collective-permute-start(bf16[2,1,128,512]{3,2,1,0:T(8,128)(2,1)S(1)} %get-tuple-element.5), channel_id=1, source_target_pairs={{4,0},{8,4},{12,8},{16,12},{20,16},{24,20},{28,24},{5,1},{9,5},{13... | collective-permute-start | bytes 786440 | tf_op jit(solution)/shard_map/ppermute | solution.py:15
  42.0 8.7 %collective-permute-start.2 = (bf16[2,1,128,512]{3,2,1,0:T(8,128)(2,1)S(1)}, bf16[2,1,128,512]{3,2,1,0:T(8,128)(2,1)S(1)}, u32[]{:S(2)}, u32[]{:S(2)}) collective-permute-start(bf16[2,1,128,512]{3,2,1,0:T(8,128)(2,1)S(1)} %get-tuple-element.6), channel_id=1, source_target_pairs={{0,4},{4,8},{8,12},{12,16},{16,20},{20,24},{24,28},{1,5},{5,9},{9,... | collective-permute-start | bytes 786440 | tf_op jit(solution)/shard_map/ppermute | solution.py:14
  62.8 390.5 %all-reduce.5.cloned.1.call-start = ((), (), s32[]{:S(2)}) async-start(), calls=%async_computation.4 | async-start | bytes 9437184 | tf_op jit(solution)/shard_map/psum | solution.py:74
  63.1 3.6 copy-start.2
  367.7 3.9 copy-start.8
  369.7 2.0 copy-start.5
  369.7 2.7 copy-start.7
  453.3 3.4 copy-start.6
Sparse Core Ops, SparseCore 0:
  28.6 168.9 reduce-scatter.4
  200.0 162.0 reduce-scatter.2
  365.5 87.8 all-reduce.4
where the time goes:
time: 465 us
  waiting for transfers between devices  369 us (79%)
  matrix products  48.3 us (10%)
  between operations  14.2 us (3%)
  starting transfers between devices  14.1 us (3%)
  other arithmetic  13 us (3%)
  local copies, waits for them, and re-layouts  6.17 us (1%)
    reduce_scatter x2, waiting for transfers between devices, settle(): lax.psum_scatter(grad_term, 'date', scatter_dimension=0, tiled=True)  289 us
    psum x1, waiting for transfers between devices, settle(): return lax.psum(share_rows, 'band')  77.7 us
    dot_general x18, matrix products, back_terms(): lax.dot_general(shifted_piece, weight[row_offset + 1, col_offset + 1], ((...  33.8 us
    dot_general x18, matrix products, weight_terms(): lax.dot_general(left_field, shifted_piece, (((0, 1, 2), (0, 1, 2)), ((),...  14.5 us
    ppermute x2, starting transfers between devices, extended(): before = lax.ppermute(last, axis, up)  10.8 us
    mul x2, other arithmetic, weight_terms(): return (stacked * grad_scale).reshape(-1, stacked.shape[2])  9.67 us
  transfers between devices with their start and end apart: 7, of which 5 were waited for; matrix products, arithmetic and copies ran while one was open for 10% of the time, Pallas kernels for 0%

commit v1 on v0

--- a/solution.py
+++ b/solution.py
@@ -70,8 +70,13 @@
 
 
 def settle(grad_term):
-    share_rows = lax.psum_scatter(grad_term, "date", scatter_dimension=0, tiled=True)
-    return lax.psum(share_rows, "band")
+    dates, bands = lax.axis_size("date"), lax.axis_size("band")
+    rows, cols = grad_term.shape
+    piece = rows // (dates * bands)
+    by_band = grad_term.reshape(dates, bands, piece, cols).swapaxes(0, 1).reshape(rows, cols)
+    share = lax.psum_scatter(by_band, "band", scatter_dimension=0, tiled=True)
+    share = lax.psum_scatter(share, "date", scatter_dimension=0, tiled=True)
+    return lax.all_gather(share, "band", axis=0, tiled=True)
 
 
 def body(inputs, preact_one, preact_two, cotangent, weight_one, weight_two):

time: 465 us -> 341 us (0.73)
  waiting for transfers between devices: 369 us -> 228 us
  local copies, waits for them, and re-layouts: 6.17 us -> 14.8 us
  matrix products: 48.3 us -> 55.6 us
    reduce_scatter x2 -> x4, waiting for transfers between devices: 289 us -> 177 us  [the longest x2 116 us: settle(): share = lax.psum_scatter(by_band, 'band', scatter_dimension=0, tiled=True)]
    psum x1 -> x0, waiting for transfers between devices: 77.7 us -> none  [settle(): return lax.psum(share_rows, 'band')]
    all_gather x0 -> x2, waiting for transfers between devices: none -> 48.4 us  [settle(): return lax.all_gather(share, 'band', axis=0, tiled=True)]
    dot_general x18, matrix products: 14.5 us -> 32.5 us  [weight_terms(): lax.dot_general(left_field, shifted_piece, (((0, 1, 2), (0, 1, 2)), ((),...]
    dot_general x18, matrix products: 33.8 us -> 23.1 us  [back_terms(): lax.dot_general(shifted_piece, weight[row_offset + 1, col_offset + 1], ((...]
    transpose x0 -> x2, local copies, waits for them, and re-layouts: none -> 9.51 us  [settle(): grad_term.reshape(dates, bands, piece, cols).swapaxes(0, 1)]
  transfers between devices with their start and end apart: 7 -> 10, of which waited for: 5 -> 8; matrix products, arithmetic and copies ran while one was open for 10% -> 14% of each run, Pallas kernels for 0% -> 0%
where the time goes in v1:
time: 341 us; the launch traced here: 340 us
  waiting for transfers between devices  228 us (67%)
  matrix products  55.6 us (16%)
  local copies, waits for them, and re-layouts  14.8 us (4%)
  between operations  14.5 us (4%)
  starting transfers between devices  13.7 us (4%)
  other arithmetic  13.3 us (4%)
    reduce_scatter x2, waiting for transfers between devices, settle(): share = lax.psum_scatter(by_band, 'band', scatter_dimension=0, tiled=True)  116 us
    reduce_scatter x2, waiting for transfers between devices, settle(): share = lax.psum_scatter(share, 'date', scatter_dimension=0, tiled=True)  61.3 us
    all_gather x2, waiting for transfers between devices, settle(): return lax.all_gather(share, 'band', axis=0, tiled=True)  48.4 us
    dot_general x18, matrix products, weight_terms(): lax.dot_general(left_field, shifted_piece, (((0, 1, 2), (0, 1, 2)), ((),...  32.5 us
    dot_general x18, matrix products, back_terms(): lax.dot_general(shifted_piece, weight[row_offset + 1, col_offset + 1], ((...  23.1 us
    ppermute x2, starting transfers between devices, extended(): before = lax.ppermute(last, axis, up)  10.3 us
    mul x2, other arithmetic, weight_terms(): return (stacked * grad_scale).reshape(-1, stacked.shape[2])  10 us
    transpose x2, local copies, waits for them, and re-layouts, settle(): grad_term.reshape(dates, bands, piece, cols).swapaxes(0, 1)  9.51 us
  transfers between devices with their start and end apart: 10, of which 8 were waited for; matrix products, arithmetic and copies ran while one was open for 14% of the time, Pallas kernels for 0%

profile of v1, /device:TPU:0, one launch (start us, length us, event | category | flops | bytes accessed | tf_op | source)
XLA Modules:
  0.0 340.1 jit_solution(716486030727833753)
XLA Ops:
  7.2 2.5 fusion.7
  11.2 3.0 collective-permute-start
  15.8 2.0 fusion.31
  21.4 2.0 fusion.28
  26.9 2.0 fusion.25
  28.9 1.9 fusion.24
  30.8 1.8 fusion.23
  32.6 4.8 %broadcast_multiply_fusion = f32[9,512,512]{2,1,0:T(8,128)S(1)} fusion(f32[9,512,512]{2,1,0:T(8,128)} %fusion.23), kind=kLoop, calls=%fused_computation.2 | loop fusion | flops 2359296 | bytes 18874368 | tf_op jit(solution)/shard_map/mul | solution.py:54
  37.5 4.8 %copy.28 = f32[8,4,144,512]{3,2,1,0:T(8,128)} copy(f32[8,4,144,512]{3,2,0,1:T(8,128)S(1)} %bitcast.311) | data formatting | bytes 18874368 | tf_op jit(solution)/shard_map/transpose | solution.py:76
  42.5 2.2 fusion.109
  44.8 1.8 fusion.43
  55.8 7.3 %collective-permute-start.2 = (bf16[2,1,128,512]{3,2,1,0:T(8,128)(2,1)S(1)}, bf16[2,1,128,512]{3,2,1,0:T(8,128)(2,1)S(1)}, u32[]{:S(2)}, u32[]{:S(2)}) collective-permute-start(bf16[2,1,128,512]{3,2,1,0:T(8,128)(2,1)S(1)} %get-tuple-element.4), channel_id=1, source_target_pairs={{0,4},{4,8},{8,12},{12,16},{16,20},{20,24},{24,28},{1,5},{5,9},{9,... | collective-permute-start | bytes 786440 | tf_op jit(solution)/shard_map/ppermute | solution.py:14
  80.7 5.2 %broadcast_multiply_fusion.1 = f32[9,512,512]{2,1,0:T(8,128)S(1)} fusion(f32[9,512,512]{2,1,0:T(8,128)} %fusion.32), kind=kLoop, calls=%fused_computation.3 | loop fusion | flops 2359296 | bytes 18874368 | tf_op jit(solution)/shard_map/mul | solution.py:54
  85.9 4.7 %copy.18 = f32[8,4,144,512]{3,2,1,0:T(8,128)} copy(f32[8,4,144,512]{3,2,0,1:T(8,128)S(1)} %bitcast.312) | data formatting | bytes 18874368 | tf_op jit(solution)/shard_map/transpose | solution.py:76
  90.7 35.9 %reduce-scatter.9.cloned.1.call-done = f32[576,512]{1,0:T(8,128)} async-done(((f32[4608,512]{1,0:T(8,128)}), f32[576,512]{1,0:T(8,128)}) %reduce-scatter.9.cloned.1.call-update) | async-done | bytes 1179664 | tf_op jit(solution)/shard_map/reduce_scatter | solution.py:77
  126.7 80.0 %reduce-scatter.5.cloned.1.call-done = f32[576,512]{1,0:T(8,128)} async-done(((f32[4608,512]{1,0:T(8,128)}), f32[576,512]{1,0:T(8,128)}) %reduce-scatter.5.cloned.1.call-update) | async-done | bytes 1179664 | tf_op jit(solution)/shard_map/reduce_scatter | solution.py:77
  206.7 31.5 %reduce-scatter.11.cloned.1.call-done = f32[144,512]{1,0:T(8,128)} async-done(((f32[576,512]{1,0:T(8,128)}), f32[144,512]{1,0:T(8,128)}) %reduce-scatter.11.cloned.1.call-update) | async-done | bytes 294928 | tf_op jit(solution)/shard_map/reduce_scatter | solution.py:78
  238.5 29.8 %reduce-scatter.7.cloned.1.call-done = f32[144,512]{1,0:T(8,128)} async-done(((f32[576,512]{1,0:T(8,128)}), f32[144,512]{1,0:T(8,128)}) %reduce-scatter.7.cloned.1.call-update) | async-done | bytes 294928 | tf_op jit(solution)/shard_map/reduce_scatter | solution.py:78
  268.3 2.2 fusion.99
  270.6 1.8 fusion.93
  278.0 2.2 add_convert_fusion
  280.2 17.6 %all-gather.5.cloned.1.call-done = f32[1152,512]{1,0:T(8,128)} async-done(((f32[144,512]{1,0:T(8,128)}), f32[1152,512]{1,0:T(8,128)}) %all-gather.5.cloned.1.call-update) | async-done | bytes 2359312 | tf_op jit(solution)/shard_map/all_gather | solution.py:79
  297.8 30.8 %all-gather.3.cloned.1.call-done = f32[1152,512]{1,0:T(8,128)} async-done(((f32[144,512]{1,0:T(8,128)}), f32[1152,512]{1,0:T(8,128)}) %all-gather.3.cloned.1.call-update) | async-done | bytes 2359312 | tf_op jit(solution)/shard_map/all_gather | solution.py:79
  328.6 3.3 copy.101
  (75 shorter events, 44.5 us)
Async XLA Ops:
  7.2 57.8 %copy-start = (bf16[2,4,128,512]{3,2,1,0:T(8,128)(2,1)S(1)}, bf16[2,4,128,512]{3,2,1,0:T(8,128)(2,1)}, u32[]{:S(2)}) copy-start(bf16[2,4,128,512]{3,2,1,0:T(8,128)(2,1)} %param.6) | copy-start | bytes 3145732
  7.2 119.4 %reduce-scatter.9.cloned.1.call-start = ((), (), s32[]{:S(2)}) async-start(), calls=%async_computation.7 | async-start | bytes 10616832 | tf_op jit(solution)/shard_map/reduce_scatter | solution.py:77
  9.7 19.2 %copy-start.3 = (bf16[2,4,128,512]{3,2,1,0:T(8,128)(2,1)}, bf16[2,4,128,512]{3,2,1,0:T(8,128)(2,1)S(1)}, u32[]{:S(2)}) copy-start(bf16[2,4,128,512]{3,2,1,0:T(8,128)(2,1)S(1)} %fusion.7) | copy-start | bytes 3145732
  9.7 6.1 %copy-start.6 = (bf16[2,4,128,512]{3,2,1,0:T(8,128)(2,1)S(1)}, bf16[2,4,128,512]{3,2,1,0:T(8,128)(2,1)}, u32[]{:S(2)}) copy-start(bf16[2,4,128,512]{3,2,1,0:T(8,128)(2,1)} %param.7) | copy-start | bytes 3145732
  9.8 4.5 %collective-permute-start.1 = (bf16[2,1,128,512]{3,2,1,0:T(8,128)(2,1)S(1)}, bf16[2,1,128,512]{3,2,1,0:T(8,128)(2,1)S(1)}, u32[]{:S(2)}, u32[]{:S(2)}) collective-permute-start(bf16[2,1,128,512]{3,2,1,0:T(8,128)(2,1)S(1)} %get-tuple-element.5), channel_id=1, source_target_pairs={{4,0},{8,4},{12,8},{16,12},{20,16},{24,20},{28,24},{5,1},{9,5},{13... | collective-permute-start | bytes 786440 | tf_op jit(solution)/shard_map/ppermute | solution.py:15
  11.2 4.2 %collective-permute-start = (bf16[2,1,128,512]{3,2,1,0:T(8,128)(2,1)S(1)}, bf16[2,1,128,512]{3,2,1,0:T(8,128)(2,1)S(1)}, u32[]{:S(2)}, u32[]{:S(2)}) collective-permute-start(bf16[2,1,128,512]{3,2,1,0:T(8,128)(2,1)S(1)} %get-tuple-element.6), channel_id=1, source_target_pairs={{0,4},{4,8},{8,12},{12,16},{16,20},{20,24},{24,28},{1,5},{5,9},{9,... | collective-permute-start | bytes 786440 | tf_op jit(solution)/shard_map/ppermute | solution.py:14
  42.3 164.4 %reduce-scatter.5.cloned.1.call-start = ((), (), s32[]{:S(2)}) async-start(), calls=%async_computation.4 | async-start | bytes 10616832 | tf_op jit(solution)/shard_map/reduce_scatter | solution.py:77
  42.5 2.3 copy-start.4
  42.5 5.9 %slice-start = ((s8[4718592]{0:T(1024)(128)(4,1)}), s8[4194304]{0:T(1024)(128)(4,1)S(1)}, s32[]{:S(2)}) async-start(s8[4718592]{0:T(1024)(128)(4,1)} %bitcast.313), calls=%async_computation.10 | async-start | bytes 8388608
  44.8 3.7 %slice-start.1 = ((s8[4718592]{0:T(1024)(128)(4,1)}), s8[524288]{0:T(1024)(128)(4,1)S(1)}, s32[]{:S(2)}) async-start(s8[4718592]{0:T(1024)(128)(4,1)} %bitcast.313), calls=%async_computation.11 | async-start | bytes 1048576
  51.5 1.2 copy-start.7
  54.4 22.9 %copy-start.1 = (bf16[2,4,128,512]{3,2,1,0:T(8,128)(2,1)}, bf16[2,4,128,512]{3,2,1,0:T(8,128)(2,1)S(1)}, u32[]{:S(2)}) copy-start(bf16[2,4,128,512]{3,2,1,0:T(8,128)(2,1)S(1)} %fusion.14) | copy-start | bytes 3145732
  54.5 8.6 %collective-permute-start.3 = (bf16[2,1,128,512]{3,2,1,0:T(8,128)(2,1)S(1)}, bf16[2,1,128,512]{3,2,1,0:T(8,128)(2,1)S(1)}, u32[]{:S(2)}, u32[]{:S(2)}) collective-permute-start(bf16[2,1,128,512]{3,2,1,0:T(8,128)(2,1)S(1)} %get-tuple-element.3), channel_id=1, source_target_pairs={{4,0},{8,4},{12,8},{16,12},{20,16},{24,20},{28,24},{5,1},{9,5},{13... | collective-permute-start | bytes 786440 | tf_op jit(solution)/shard_map/ppermute | solution.py:15
  55.8 8.8 %collective-permute-start.2 = (bf16[2,1,128,512]{3,2,1,0:T(8,128)(2,1)S(1)}, bf16[2,1,128,512]{3,2,1,0:T(8,128)(2,1)S(1)}, u32[]{:S(2)}, u32[]{:S(2)}) collective-permute-start(bf16[2,1,128,512]{3,2,1,0:T(8,128)(2,1)S(1)} %get-tuple-element.4), channel_id=1, source_target_pairs={{0,4},{4,8},{8,12},{12,16},{16,20},{20,24},{24,28},{1,5},{5,9},{9,... | collective-permute-start | bytes 786440 | tf_op jit(solution)/shard_map/ppermute | solution.py:14
  90.7 147.5 %reduce-scatter.11.cloned.1.call-start = ((), (), s32[]{:S(2)}) async-start(), calls=%async_computation.8 | async-start | bytes 1474560 | tf_op jit(solution)/shard_map/reduce_scatter | solution.py:78
  126.6 141.6 %reduce-scatter.7.cloned.1.call-start = ((), (), s32[]{:S(2)}) async-start(), calls=%async_computation.5 | async-start | bytes 1474560 | tf_op jit(solution)/shard_map/reduce_scatter | solution.py:78
  206.7 91.1 %all-gather.5.cloned.1.call-start = ((), (), s32[]{:S(2)}) async-start(), calls=%async_computation.9 | async-start | bytes 2654208 | tf_op jit(solution)/shard_map/all_gather | solution.py:79
  238.2 90.3 %all-gather.3.cloned.1.call-start = ((), (), s32[]{:S(2)}) async-start(), calls=%async_computation.6 | async-start | bytes 2654208 | tf_op jit(solution)/shard_map/all_gather | solution.py:79
  268.3 2.3 copy-start.2
  268.3 5.9 %slice-start.2 = ((s8[4718592]{0:T(1024)(128)(4,1)}), s8[4194304]{0:T(1024)(128)(4,1)S(1)}, s32[]{:S(2)}) async-start(s8[4718592]{0:T(1024)(128)(4,1)} %bitcast.315), calls=%async_computation.12 | async-start | bytes 8388608
  270.6 3.7 %slice-start.3 = ((s8[4718592]{0:T(1024)(128)(4,1)}), s8[524288]{0:T(1024)(128)(4,1)S(1)}, s32[]{:S(2)}) async-start(s8[4718592]{0:T(1024)(128)(4,1)} %bitcast.315), calls=%async_computation.13 | async-start | bytes 1048576
  297.8 34.1 %copy-start.5 = (f32[1152,512]{1,0:T(8,128)S(1)}, f32[1152,512]{1,0:T(8,128)}, u32[]{:S(2)}) copy-start(f32[1152,512]{1,0:T(8,128)} %all-gather.5.cloned.1.call-done) | copy-start | bytes 7077892
Sparse Core Ops, SparseCore 0:
  42.4 84.1 reduce-scatter.8
  130.1 76.4 reduce-scatter.4
  209.0 29.1 reduce-scatter.10
  240.4 27.8 reduce-scatter.6
  270.0 27.7 all-gather.4
  299.5 29.0 all-gather.2

commit v2 on v1

--- a/solution.py
+++ b/solution.py
@@ -74,8 +74,8 @@
     rows, cols = grad_term.shape
     piece = rows // (dates * bands)
     by_band = grad_term.reshape(dates, bands, piece, cols).swapaxes(0, 1).reshape(rows, cols)
-    share = lax.psum_scatter(by_band, "band", scatter_dimension=0, tiled=True)
-    share = lax.psum_scatter(share, "date", scatter_dimension=0, tiled=True)
+    share = lax.psum_scatter(by_band.astype(jnp.bfloat16), "band", scatter_dimension=0, tiled=True)
+    share = lax.psum_scatter(share.astype(jnp.float32), "date", scatter_dimension=0, tiled=True)
     return lax.all_gather(share, "band", axis=0, tiled=True)
 
 

time: 341 us -> 282 us (0.83)
  waiting for transfers between devices: 228 us -> 193 us
  matrix products: 55.6 us -> 39.9 us
    reduce_scatter x4, waiting for transfers between devices: 177 us -> 144 us  [the longest x2 83.3 us: settle(): lax.psum_scatter(by_band.astype(jnp.bfloat16), 'band', scatter_dimension=...]
    dot_general x18, matrix products: 32.5 us -> 14.5 us  [weight_terms(): lax.dot_general(left_field, shifted_piece, (((0, 1, 2), (0, 1, 2)), ((),...]
    mul x2 -> x0, other arithmetic: 10 us -> none  [weight_terms(): return (stacked * grad_scale).reshape(-1, stacked.shape[2])]
    transpose x2 -> x0, local copies, waits for them, and re-layouts: 9.51 us -> none  [settle(): grad_term.reshape(dates, bands, piece, cols).swapaxes(0, 1)]
    convert_element_type x0 -> x4, other arithmetic: none -> 7.46 us  [the longest x2 4.46 us: settle(): share.astype(jnp.float32)]
    convert_element_type x0 -> x2, local copies, waits for them, and re-layouts: none -> 5.22 us  [settle(): by_band.astype(jnp.bfloat16)]
  transfers between devices with their start and end apart: 10 -> 10, of which waited for: 8 -> 7; matrix products, arithmetic and copies ran while one was open for 14% -> 15% of each run, Pallas kernels for 0% -> 0%
where the time goes in v2:
time: 282 us
  waiting for transfers between devices  193 us (68%)
  matrix products  39.9 us (14%)
  between operations  14.6 us (5%)
  local copies, waits for them, and re-layouts  12.1 us (4%)
  starting transfers between devices  11.4 us (4%)
  other arithmetic  10.8 us (4%)
    reduce_scatter x2, waiting for transfers between devices, settle(): lax.psum_scatter(by_band.astype(jnp.bfloat16), 'band', scatter_dimension=...  83.3 us
    reduce_scatter x2, waiting for transfers between devices, settle(): lax.psum_scatter(share.astype(jnp.float32), 'date', scatter_dimension=0,...  60.2 us
    all_gather x2, waiting for transfers between devices, settle(): return lax.all_gather(share, 'band', axis=0, tiled=True)  48.4 us
    dot_general x18, matrix products, back_terms(): lax.dot_general(shifted_piece, weight[row_offset + 1, col_offset + 1], ((...  25.4 us
    dot_general x18, matrix products, weight_terms(): lax.dot_general(left_field, shifted_piece, (((0, 1, 2), (0, 1, 2)), ((),...  14.5 us
    ppermute x2, starting transfers between devices, extended(): before = lax.ppermute(last, axis, up)  8.22 us
    unnamed x28, local copies, waits for them, and re-layouts  6.76 us
  transfers between devices with their start and end apart: 10, of which 7 were waited for; matrix products, arithmetic and copies ran while one was open for 15% of the time, Pallas kernels for 0%

profile of v2, /device:TPU:0, one launch (start us, length us, event | category | flops | bytes accessed | tf_op | source)
XLA Modules:
  0.0 281.8 jit_solution(16105556606031630167)
XLA Ops:
  7.2 2.5 fusion.7
  11.1 3.0 %collective-permute-start = (bf16[2,1,128,512]{3,2,1,0:T(8,128)(2,1)S(1)}, bf16[2,1,128,512]{3,2,1,0:T(8,128)(2,1)S(1)}, u32[]{:S(2)}, u32[]{:S(2)}) collective-permute-start(bf16[2,1,128,512]{3,2,1,0:T(8,128)(2,1)S(1)} %get-tuple-element.6), channel_id=1, source_target_pairs={{0,4},{4,8},{8,12},{12,16},{16,20},{20,24},{24,28},{1,5},{5,9},{9,... | collective-permute-start | bytes 786440 | tf_op jit(solution)/shard_map/ppermute | solution.py:14
  14.1 3.1 %fusion.109 = f32[2,4,128,512]{3,2,1,0:T(8,128)} fusion(bf16[2,4,128,512]{3,2,1,0:T(8,128)(2,1)S(1)} %fusion.7, bf16[3,3,512,512]{3,2,1,0:T(8,128)(2,1)} %param.11), kind=kOutput, calls=%fused_computation.137 | convolution fusion | flops 536870912 | bytes 3670016 | tf_op jit(solution)/shard_map/dot_general | solution.py:62
  26.2 1.5 multiply_convert_fusion
  27.7 2.6 copy.28
  30.6 2.2 fusion.43
  32.8 1.8 fusion.39
  34.7 1.8 fusion.79
  40.6 1.7 fusion.14
  43.7 5.2 %collective-permute-start.2 = (bf16[2,1,128,512]{3,2,1,0:T(8,128)(2,1)S(1)}, bf16[2,1,128,512]{3,2,1,0:T(8,128)(2,1)S(1)}, u32[]{:S(2)}, u32[]{:S(2)}) collective-permute-start(bf16[2,1,128,512]{3,2,1,0:T(8,128)(2,1)S(1)} %get-tuple-element.4), channel_id=1, source_target_pairs={{0,4},{4,8},{8,12},{12,16},{16,20},{20,24},{24,28},{1,5},{5,9},{9,... | collective-permute-start | bytes 786440 | tf_op jit(solution)/shard_map/ppermute | solution.py:14
  58.8 2.6 copy.18
  61.5 27.9 %reduce-scatter.9.cloned.1.call-done = bf16[576,512]{1,0:T(8,128)(2,1)} async-done(((bf16[4608,512]{1,0:T(8,128)(2,1)}), bf16[576,512]{1,0:T(8,128)(2,1)}) %reduce-scatter.9.cloned.1.call-update) | async-done | bytes 589840 | tf_op jit(solution)/shard_map/reduce_scatter | solution.py:77
  89.4 2.2 convert_element_type.71
  91.7 55.4 %reduce-scatter.5.cloned.1.call-done = bf16[576,512]{1,0:T(8,128)(2,1)} async-done(((bf16[4608,512]{1,0:T(8,128)(2,1)}), bf16[576,512]{1,0:T(8,128)(2,1)}) %reduce-scatter.5.cloned.1.call-update) | async-done | bytes 589840 | tf_op jit(solution)/shard_map/reduce_scatter | solution.py:77
  147.1 2.2 convert_element_type.65
  149.4 29.8 %reduce-scatter.11.cloned.1.call-done = f32[144,512]{1,0:T(8,128)} async-done(((f32[576,512]{1,0:T(8,128)}), f32[144,512]{1,0:T(8,128)}) %reduce-scatter.11.cloned.1.call-update) | async-done | bytes 294928 | tf_op jit(solution)/shard_map/reduce_scatter | solution.py:78
  179.5 30.4 %reduce-scatter.7.cloned.1.call-done = f32[144,512]{1,0:T(8,128)} async-done(((f32[576,512]{1,0:T(8,128)}), f32[144,512]{1,0:T(8,128)}) %reduce-scatter.7.cloned.1.call-update) | async-done | bytes 294928 | tf_op jit(solution)/shard_map/reduce_scatter | solution.py:78
  209.9 2.2 fusion.99
  212.2 1.8 fusion.93
  214.0 1.8 fusion.94
  219.6 2.2 add_convert_fusion
  221.8 17.6 %all-gather.5.cloned.1.call-done = f32[1152,512]{1,0:T(8,128)} async-done(((f32[144,512]{1,0:T(8,128)}), f32[1152,512]{1,0:T(8,128)}) %all-gather.5.cloned.1.call-update) | async-done | bytes 2359312 | tf_op jit(solution)/shard_map/all_gather | solution.py:79
  239.4 30.8 %all-gather.3.cloned.1.call-done = f32[1152,512]{1,0:T(8,128)} async-done(((f32[144,512]{1,0:T(8,128)}), f32[1152,512]{1,0:T(8,128)}) %all-gather.3.cloned.1.call-update) | async-done | bytes 2359312 | tf_op jit(solution)/shard_map/all_gather | solution.py:79
  270.2 3.4 %copy.101 = f32[1152,512]{1,0:T(8,128)} copy(f32[1152,512]{1,0:T(8,128)} %all-gather.3.cloned.1.call-done) | data formatting | bytes 4718592
  (79 shorter events, 31.5 us)
Async XLA Ops:
  7.2 43.3 %copy-start = (bf16[2,4,128,512]{3,2,1,0:T(8,128)(2,1)S(1)}, bf16[2,4,128,512]{3,2,1,0:T(8,128)(2,1)}, u32[]{:S(2)}) copy-start(bf16[2,4,128,512]{3,2,1,0:T(8,128)(2,1)} %param.6) | copy-start | bytes 3145732
  7.2 82.2 %reduce-scatter.9.cloned.1.call-start = ((), (), s32[]{:S(2)}) async-start(), calls=%async_computation.7 | async-start | bytes 5308416 | tf_op jit(solution)/shard_map/reduce_scatter | solution.py:77
  9.7 15.0 %copy-start.3 = (bf16[2,4,128,512]{3,2,1,0:T(8,128)(2,1)}, bf16[2,4,128,512]{3,2,1,0:T(8,128)(2,1)S(1)}, u32[]{:S(2)}) copy-start(bf16[2,4,128,512]{3,2,1,0:T(8,128)(2,1)S(1)} %fusion.7) | copy-start | bytes 3145732
  9.8 7.5 %collective-permute-start.1 = (bf16[2,1,128,512]{3,2,1,0:T(8,128)(2,1)S(1)}, bf16[2,1,128,512]{3,2,1,0:T(8,128)(2,1)S(1)}, u32[]{:S(2)}, u32[]{:S(2)}) collective-permute-start(bf16[2,1,128,512]{3,2,1,0:T(8,128)(2,1)S(1)} %get-tuple-element.5), channel_id=1, source_target_pairs={{4,0},{8,4},{12,8},{16,12},{20,16},{24,20},{28,24},{5,1},{9,5},{13... | collective-permute-start | bytes 786440 | tf_op jit(solution)/shard_map/ppermute | solution.py:15
  11.1 6.2 %collective-permute-start = (bf16[2,1,128,512]{3,2,1,0:T(8,128)(2,1)S(1)}, bf16[2,1,128,512]{3,2,1,0:T(8,128)(2,1)S(1)}, u32[]{:S(2)}, u32[]{:S(2)}) collective-permute-start(bf16[2,1,128,512]{3,2,1,0:T(8,128)(2,1)S(1)} %get-tuple-element.6), channel_id=1, source_target_pairs={{0,4},{4,8},{8,12},{12,16},{16,20},{20,24},{24,28},{1,5},{5,9},{9,... | collective-permute-start | bytes 786440 | tf_op jit(solution)/shard_map/ppermute | solution.py:14
  17.2 1.2 copy-start.7
  30.4 116.7 %reduce-scatter.5.cloned.1.call-start = ((), (), s32[]{:S(2)}) async-start(), calls=%async_computation.4 | async-start | bytes 5308416 | tf_op jit(solution)/shard_map/reduce_scatter | solution.py:77
  30.6 2.2 copy-start.4
  30.6 5.9 %slice-start = ((s8[4718592]{0:T(1024)(128)(4,1)}), s8[4194304]{0:T(1024)(128)(4,1)S(1)}, s32[]{:S(2)}) async-start(s8[4718592]{0:T(1024)(128)(4,1)} %bitcast.313), calls=%async_computation.10 | async-start | bytes 8388608
  32.8 3.7 %slice-start.1 = ((s8[4718592]{0:T(1024)(128)(4,1)}), s8[524288]{0:T(1024)(128)(4,1)S(1)}, s32[]{:S(2)}) async-start(s8[4718592]{0:T(1024)(128)(4,1)} %bitcast.313), calls=%async_computation.11 | async-start | bytes 1048576
  38.7 1.6 copy-start.5
  38.8 1.8 copy-start.8
  42.3 13.5 %copy-start.1 = (bf16[2,4,128,512]{3,2,1,0:T(8,128)(2,1)}, bf16[2,4,128,512]{3,2,1,0:T(8,128)(2,1)S(1)}, u32[]{:S(2)}) copy-start(bf16[2,4,128,512]{3,2,1,0:T(8,128)(2,1)S(1)} %fusion.14) | copy-start | bytes 3145732
  42.4 6.5 %collective-permute-start.3 = (bf16[2,1,128,512]{3,2,1,0:T(8,128)(2,1)S(1)}, bf16[2,1,128,512]{3,2,1,0:T(8,128)(2,1)S(1)}, u32[]{:S(2)}, u32[]{:S(2)}) collective-permute-start(bf16[2,1,128,512]{3,2,1,0:T(8,128)(2,1)S(1)} %get-tuple-element.3), channel_id=1, source_target_pairs={{4,0},{8,4},{12,8},{16,12},{20,16},{24,20},{28,24},{5,1},{9,5},{13... | collective-permute-start | bytes 786440 | tf_op jit(solution)/shard_map/ppermute | solution.py:15
  43.7 6.3 %collective-permute-start.2 = (bf16[2,1,128,512]{3,2,1,0:T(8,128)(2,1)S(1)}, bf16[2,1,128,512]{3,2,1,0:T(8,128)(2,1)S(1)}, u32[]{:S(2)}, u32[]{:S(2)}) collective-permute-start(bf16[2,1,128,512]{3,2,1,0:T(8,128)(2,1)S(1)} %get-tuple-element.4), channel_id=1, source_target_pairs={{0,4},{4,8},{8,12},{12,16},{16,20},{20,24},{24,28},{1,5},{5,9},{9,... | collective-permute-start | bytes 786440 | tf_op jit(solution)/shard_map/ppermute | solution.py:14
  61.4 117.8 %reduce-scatter.11.cloned.1.call-start = ((), (), s32[]{:S(2)}) async-start(), calls=%async_computation.8 | async-start | bytes 1474560 | tf_op jit(solution)/shard_map/reduce_scatter | solution.py:78
  91.6 118.3 %reduce-scatter.7.cloned.1.call-start = ((), (), s32[]{:S(2)}) async-start(), calls=%async_computation.5 | async-start | bytes 1474560 | tf_op jit(solution)/shard_map/reduce_scatter | solution.py:78
  149.4 90.0 %all-gather.5.cloned.1.call-start = ((), (), s32[]{:S(2)}) async-start(), calls=%async_computation.9 | async-start | bytes 2654208 | tf_op jit(solution)/shard_map/all_gather | solution.py:79
  179.2 90.9 %all-gather.3.cloned.1.call-start = ((), (), s32[]{:S(2)}) async-start(), calls=%async_computation.6 | async-start | bytes 2654208 | tf_op jit(solution)/shard_map/all_gather | solution.py:79
  209.9 2.3 copy-start.2
  209.9 5.9 %slice-start.2 = ((s8[4718592]{0:T(1024)(128)(4,1)}), s8[4194304]{0:T(1024)(128)(4,1)S(1)}, s32[]{:S(2)}) async-start(s8[4718592]{0:T(1024)(128)(4,1)} %bitcast.315), calls=%async_computation.12 | async-start | bytes 8388608
  212.2 3.7 %slice-start.3 = ((s8[4718592]{0:T(1024)(128)(4,1)}), s8[524288]{0:T(1024)(128)(4,1)S(1)}, s32[]{:S(2)}) async-start(s8[4718592]{0:T(1024)(128)(4,1)} %bitcast.315), calls=%async_computation.13 | async-start | bytes 1048576
  270.2 3.4 %copy-start.6 = (f32[1152,512]{1,0:T(8,128)S(1)}, f32[1152,512]{1,0:T(8,128)}, u32[]{:S(2)}) copy-start(f32[1152,512]{1,0:T(8,128)} %all-gather.5.cloned.1.call-done) | copy-start | bytes 7077892
Sparse Core Ops, SparseCore 0:
  30.5 58.8 reduce-scatter.8
  93.2 53.8 reduce-scatter.4
  150.0 29.1 reduce-scatter.10
  182.0 27.8 reduce-scatter.6
  211.6 27.7 all-gather.4
  241.1 29.0 all-gather.2
